TPU v7x, 256 devices: a whole 4x4x8 slice. The times are simulated.
256 devices in a mesh: seq: 32 (over z, y), dp: 8 (over x, core).
Axes of the slice: x: 4, y: 4, z: 8, core: 2. Of those that a mesh axis runs over, the one named last changes fastest.
Arguments:
- queries: bfloat16 [8, 12288, 2048], P('dp', 'seq'), may hold values from -0.59765625 to 0.59765625
- keys: bfloat16 [8, 12288, 2048], P('dp', 'seq'), may hold values from -0.59765625 to 0.59765625
- values: bfloat16 [8, 12288, 2048], P('dp', 'seq'), may hold values from -6 to 6
- output_gradient: bfloat16 [8, 12288, 2048], P('dp', 'seq'), may hold values from -0.59765625 to 0.59765625
- document_lengths: int32 [8, 8], P('dp'), may hold values from 1 to 3072, 12288 in all within a row
- cutoff_rows: int32 [8, 12288], P('dp', 'seq'), may hold values 0 or 1
- head_decay_rate: float32 [16], replicated, may hold values from 4.06901042e-06 to 0.04, as said below
Outputs:
- query_grad: bfloat16 [8, 12288, 2048], P('dp', 'seq')
- key_grad: bfloat16 [8, 12288, 2048], P('dp', 'seq')
- value_grad: bfloat16 [8, 12288, 2048], P('dp', 'seq')
- rate_grad: float32 [16], replicated
Inputs may be any that keep to these rules, and one draw needn't show every extreme that they name: `head_decay_rate`: a positive rate for each head.
All inputs are finite; a program needn't handle non-finite values. No bound on the sum of `cutoff_rows` on one device may be relied on, other than what follows from the above.
Results may differ from a plain program's by a relative error of at most 0.0034.
Values sent between devices are 32-bit elements; how exact they have to be, the bound alone decides.
No kernel may reach another device: no remote copies, remote signals or barrier semaphores. Data moves between devices by JAX's collectives and lax.ppermute only.
A program may use at most 192 MiB of HBM per device.

v0:
```python
import math
import jax
import jax.numpy as jnp
from jax import lax
from jax.sharding import PartitionSpec as P

HEADS = 16
HEAD_DIM = 128
cutoff_logarithm = math.log(0.7)
state_mode = lax.Precision.HIGH


def carried_in(part, axis, combine, identity, reverse):
    count = lax.axis_size(axis)
    place = lax.axis_index(axis)
    ahead = count - 1 - place if reverse else place
    gathered = jax.tree.map(lambda a: lax.all_gather(a, axis), part)
    state = jax.tree.map(lambda a, e: jnp.zeros_like(a) + jnp.asarray(e, a.dtype), part, identity)

    def one(step, state):
        source = count - 1 - step if reverse else step
        return combine(
            state, jax.tree.map(lambda a: lax.dynamic_index_in_dim(a, source, 0, False), gathered)
        )

    return lax.fori_loop(0, ahead, one, state)


def block_mask_list(head_decay_rate, cutoff_list, row_position, start_list):
    is_start = jnp.any(row_position[:, None] == start_list[None, :], axis=1)
    seg_local = jnp.cumsum(is_start.astype(jnp.int32))
    begin = jnp.max(
        jnp.where(start_list[None, :] <= row_position[:, None], start_list[None, :], 0), axis=1
    )
    position = (row_position - begin).astype(jnp.float32)
    logarithm_step = (
        cutoff_list.astype(jnp.float32)[:, None] * cutoff_logarithm - head_decay_rate[None, :]
    )
    cum_log = jnp.cumsum(logarithm_step, axis=0)
    carry_in = jnp.where((seg_local == 0)[:, None], jnp.exp(cum_log), 0.0)
    carry_out = jnp.where(
        (seg_local == seg_local[-1])[:, None], jnp.exp(cum_log[-1][None, :] - cum_log), 0.0
    )
    decay_all = jnp.where(seg_local[-1] == 0, jnp.exp(cum_log[-1]), 0.0)
    return (cum_log, seg_local, position, carry_in, carry_out, decay_all)


def weights_of(cum_log, seg_local):
    count = seg_local.shape[0]
    index = jnp.arange(count, dtype=jnp.int32)
    allowed = (seg_local[:, None] == seg_local[None, :]) & (index[:, None] >= index[None, :])
    spread = cum_log.T[:, :, None] - cum_log.T[:, None, :]
    return jnp.where(allowed[None], jnp.exp(jnp.where(allowed[None], spread, 0.0)), 0.0)


def forward_combine(earlier, later):
    return (earlier[0] * later[0], later[0][:, None, None] * earlier[1] + later[1])


def backward_combine(earlier, later):
    return (later[0] * earlier[0], later[1] + later[0][:, None, None] * earlier[1])


def on_device(
    queries, keys, values, output_gradient, document_lengths, cutoff_rows, head_decay_rate
):
    row_count = queries.shape[1]
    query_block = queries.reshape(row_count, HEADS, HEAD_DIM)
    key_block = keys.reshape(row_count, HEADS, HEAD_DIM)
    value_block = values.reshape(row_count, HEADS, HEAD_DIM)
    gradient_block = output_gradient.reshape(row_count, HEADS, HEAD_DIM)
    block_piece = lax.axis_index("seq")
    row_position = block_piece * row_count + jnp.arange(row_count, dtype=jnp.int32)
    length_list = document_lengths[0]
    start_list = jnp.cumsum(length_list) - length_list
    cum_log, seg_local, position, carry_in, carry_out, decay_all = block_mask_list(
        head_decay_rate, cutoff_rows[0], row_position, start_list
    )
    key_f = key_block.astype(jnp.float32)
    value_f = value_block.astype(jnp.float32)
    grad_f = gradient_block.astype(jnp.float32)
    query_f = query_block.astype(jnp.float32)
    state_local = jnp.einsum(
        "the,thf->hef", carry_out[:, :, None] * key_f, value_f, precision=state_mode
    )
    back_local = jnp.einsum(
        "she,shf->hef", carry_in[:, :, None] * query_f, grad_f, precision=state_mode
    )
    identity = (jnp.ones_like(decay_all), jnp.zeros_like(state_local))
    state_input = carried_in((decay_all, state_local), "seq", forward_combine, identity, False)[1]
    backward_input = carried_in((decay_all, back_local), "seq", backward_combine, identity, True)[1]
    weight = weights_of(cum_log, seg_local)
    scores = jnp.einsum("she,the->hst", query_block, key_block, preferred_element_type=jnp.float32)
    grad_scores = jnp.einsum(
        "shf,thf->hst", gradient_block, value_block, preferred_element_type=jnp.float32
    )
    attn_prob = (weight * scores).astype(jnp.bfloat16)
    grad_prob = (weight * grad_scores).astype(jnp.bfloat16)
    value_full = jnp.einsum(
        "hst,shf->thf", attn_prob, gradient_block, preferred_element_type=jnp.float32
    )
    value_full = value_full + carry_out[:, :, None] * jnp.einsum(
        "the,hef->thf", key_f, backward_input, precision=state_mode
    )
    query_full = jnp.einsum(
        "hst,the->she", grad_prob, key_block, preferred_element_type=jnp.float32
    )
    query_full = query_full + carry_in[:, :, None] * jnp.einsum(
        "shf,hef->she", grad_f, state_input, precision=state_mode
    )
    key_full = jnp.einsum(
        "hst,she->the", grad_prob, query_block, preferred_element_type=jnp.float32
    )
    key_full = key_full + carry_out[:, :, None] * jnp.einsum(
        "thf,hef->the", value_f, backward_input, precision=state_mode
    )
    inner_step = jnp.sum(key_f * key_full, axis=2) - jnp.sum(query_f * query_full, axis=2)
    rate_part = jnp.sum(position[:, None] * inner_step, axis=0)
    rate_total = lax.psum(rate_part, ("seq", "dp"))
    token_total = row_count * lax.axis_size("seq") * lax.axis_size("dp")
    rate_grad = head_decay_rate * rate_total / math.sqrt(token_total)
    out_shape = (1, row_count, HEADS * HEAD_DIM)
    return (
        query_full.astype(jnp.bfloat16).reshape(out_shape),
        key_full.astype(jnp.bfloat16).reshape(out_shape),
        value_full.astype(jnp.bfloat16).reshape(out_shape),
        rate_grad,
    )


def solution(mesh):
    in_specs = (
        P("dp", "seq", None),
        P("dp", "seq", None),
        P("dp", "seq", None),
        P("dp", "seq", None),
        P("dp", None),
        P("dp", "seq"),
        P(),
    )
    out_specs = (P("dp", "seq", None), P("dp", "seq", None), P("dp", "seq", None), P())
    return jax.shard_map(
        on_device, mesh=mesh, in_specs=in_specs, out_specs=out_specs, check_vma=False
    )
```

profile of v0, /device:TPU:1, one launch (start us, length us, event | category | flops | bytes accessed | tf_op | source)
XLA Modules:
  0.0 647.6 jit_solution(15343796747295576941)
XLA Ops:
  13.9 1.9 copy.84
  15.8 2.4 copy.99
  18.5 2.4 fusion.9
  21.0 1.9 copy.81
  22.8 1.8 copy.101
  25.8 2.4 fusion.7
  28.2 38.4 %all-gather.2 = f32[32,1,16]{2,1,0:T(1,128)S(1)} all-gather(f32[1,1,16]{2,1,0:T(1,128)S(1)} %bitcast.115), channel_id=1, replica_groups=mesh['seq'=32,'dp'=8] {'seq'}, dimensions={0}, use_global_device_ids=true | all-gather | bytes 2112 | tf_op jit(solution)/shard_map/all_gather | solution.py:17
  66.9 6.9 %multiply_convert_fusion.1 = bf16[16,384,384]{2,1,0:T(8,128)(2,1)} fusion(f32[16,384]{1,0:T(8,128)S(1)} %get-tuple-element.184, pred[384,384]{1,0:T(8,128)(4,1)S(1)} %fusion.21, bf16[384,16,128]{0,2,1:T(8,128)(2,1)S(1)} %bitcast.99, bf16[384,16,128]{2,1,0:T(8,128)(2,1)} %bitcast.103), kind=kOutput, calls=%fused_computation.5 | convolution fusion | flops 615776256 | bytes 8036352 | tf_op jit(solution)/shard_map/shf,thf->hst/dot_general | solution.py:94
  73.8 184.0 %all-gather.8.cloned.1.call-done = f32[512,128,128]{2,1,0:T(8,128)} async-done(((f32[16,128,128]{2,1,0:T(8,128)}), f32[512,128,128]{2,1,0:T(8,128)}) %all-gather.8.cloned.1.call-update) | async-done | bytes 33554448 | tf_op jit(solution)/shard_map/all_gather | solution.py:17
  257.9 46.7 %while.27 = (s32[]{:T(128)}, f32[16,128,128]{2,1,0:T(8,128)S(1)}, s32[]{:T(128)}, f32[32,16,128,128]{3,2,1,0:T(8,128)}, f32[32,16]{1,0:T(8,128)S(1)}, /*index=5*/s32[]{:T(128)}, s32[]{:T(128)}, s32[]{:T(128)}, s32[]{:T(128)}) while((s32[]{:T(128)}, f32[16,128,128]{2,1,0:T(8,128)S(1)}, s32[]{:T(128)}, f32[32,16,128,128]{3,2,1,0:T(8,128)}, ...), condition=%wide.region_9.10_spmd, body=%wide.region_8.9_spmd.sunk | while | flops 524294 | bytes 3146075 | solution.py:26
  257.9 1.4 bitcast_add_fusion.5
  259.4 1.4 bitcast_add_fusion.5
  260.9 1.4 bitcast_add_fusion.5
  262.4 1.4 bitcast_add_fusion.5
  263.9 1.4 bitcast_add_fusion.5
  265.4 1.4 bitcast_add_fusion.5
  266.9 1.4 bitcast_add_fusion.5
  268.4 1.4 bitcast_add_fusion.5
  269.9 1.6 bitcast_add_fusion.5
  271.5 1.5 bitcast_add_fusion.5
  273.1 1.4 bitcast_add_fusion.5
  274.6 1.4 bitcast_add_fusion.5
  276.0 1.4 bitcast_add_fusion.5
  277.5 1.5 bitcast_add_fusion.5
  279.1 1.5 bitcast_add_fusion.5
  280.6 1.5 bitcast_add_fusion.5
  282.1 1.5 bitcast_add_fusion.5
  283.6 1.5 bitcast_add_fusion.5
  285.1 1.5 bitcast_add_fusion.5
  286.6 1.5 bitcast_add_fusion.5
  288.1 1.5 bitcast_add_fusion.5
  295.6 1.5 bitcast_add_fusion.5
  297.1 1.5 bitcast_add_fusion.5
  298.6 1.5 bitcast_add_fusion.5
  300.1 1.5 bitcast_add_fusion.5
  301.6 1.5 bitcast_add_fusion.5
  303.2 1.5 bitcast_add_fusion.5
  304.6 4.5 fusion.17
  309.2 2.7 fusion.25
  311.8 178.9 %all-gather.6.cloned.1.call-done = f32[512,128,128]{2,1,0:T(8,128)} async-done(((f32[16,128,128]{2,1,0:T(8,128)}), f32[512,128,128]{2,1,0:T(8,128)}) %all-gather.6.cloned.1.call-update) | async-done | bytes 33554448 | tf_op jit(solution)/shard_map/all_gather | solution.py:17
  491.1 4.0 fusion.24
  495.1 8.2 %fusion.12 = bf16[384,16,128]{0,2,1:T(8,128)(2,1)} fusion(f32[16,128,384]{2,1,0:T(8,128)} %fusion.25, bf16[384,16,128]{0,2,1:T(8,128)(2,1)} %bitcast.101, f32[16,384]{1,0:T(8,128)S(1)} %get-tuple-element.184, pred[384,384]{1,0:T(8,128)(4,1)S(1)} %fusion.21, bf16[384,16,128]{0,2,1:T(8,128)(2,1)} %bitcast.95, bf16[384,16,128]{0,2,1:T(8,128)(2,1)S(1)} %bitcast.91, ...), kind=kOutput, calls=%fused_computation.23 | convolution fusion | flops 1222115328 | bytes 9633792 | tf_op jit(solution)/shard_map/hst,shf->thf/dot_general | solution.py:99
  503.3 2.7 copy.94
  506.0 5.9 fusion.8
  512.0 5.1 fusion.10
  517.2 2.7 copy.92
  519.9 118.8 %psum.7 = f32[16]{0:T(128)S(1)} all-reduce(f32[16]{0:T(128)S(1)} %multiply_reduce_fusion), channel_id=1, replica_groups=mesh['seq'=32,'dp'=8] {'seq','dp'}, use_global_device_ids=true, to_apply=%region_14.15 | all-reduce | flops 16 | bytes 128 | tf_op jit(solution)/shard_map/psum | solution.py:119
  639.2 1.6 copy.93
  (81 shorter events, 14.9 us)
Async XLA Ops:
  7.2 250.6 %all-gather.8.cloned.1.call-start = ((), (), s32[]{:S(2)}) async-start(), calls=%async_computation.1 | async-start | bytes 34603008 | tf_op jit(solution)/shard_map/all_gather | solution.py:17
  15.8 5.1 copy-start
  18.2 48.7 %copy-start.2 = (bf16[1,384,2048]{1,2,0:T(8,128)(2,1)}, bf16[1,384,2048]{1,2,0:T(8,128)(2,1)S(1)}, u32[]{:S(2)}) copy-start(bf16[1,384,2048]{1,2,0:T(8,128)(2,1)S(1)} %copy.99) | copy-start | bytes 4718596
  20.9 469.8 %all-gather.6.cloned.1.call-start = ((), (), s32[]{:S(2)}) async-start(), calls=%async_computation | async-start | bytes 34603008 | tf_op jit(solution)/shard_map/all_gather | solution.py:17
  24.7 1.1 copy-start.3
  503.3 2.7 copy-start.1
  506.0 5.9 copy-start.4
  517.1 121.6 %copy-start.6 = (f32[16]{0:T(128)S(1)}, f32[16]{0:T(128)}, u32[]{:S(2)}) copy-start(f32[16]{0:T(128)} %param.17) | copy-start | bytes 196
  517.1 122.1 %copy-start.5 = (bf16[384,16,128]{0,2,1:T(8,128)(2,1)S(1)}, bf16[384,16,128]{0,2,1:T(8,128)(2,1)}, u32[]{:S(2)}) copy-start(bf16[384,16,128]{0,2,1:T(8,128)(2,1)} %get-tuple-element.181) | copy-start | bytes 4718596
Sparse Core Ops, SparseCore 0:
  21.0 236.7 all-gather.7
  260.4 230.3 all-gather.5
where the time goes:
time: 649 us; the launch traced here: 648 us
  waiting for transfers between devices  363 us (56%)
  blocking collectives  157 us (24%)
  other arithmetic  51.5 us (8%)
  matrix products  42 us (6%)
  local copies, waits for them, and re-layouts  17.7 us (3%)
  between operations  14.8 us (2%)
    all_gather x2, waiting for transfers between devices, carried_in(): gathered = jax.tree.map(lambda a: lax.all_gather(a, axis), part)  363 us
    psum x1, blocking collectives, on_device(): rate_total = lax.psum(rate_part, ('seq', 'dp'))  119 us
    add x31, other arithmetic, backward_combine(): later[1] + later[0][:, None, None] * earlier[1]  45.3 us
    all_gather x1, blocking collectives, carried_in(): gathered = jax.tree.map(lambda a: lax.all_gather(a, axis), part)  38.4 us
    unnamed x20, local copies, waits for them, and re-layouts  13.7 us
  transfers between devices with their start and end apart: 2, of which 2 were waited for; matrix products, arithmetic and copies ran while one was open for 10% of the time, Pallas kernels for 0%

commit v1 on v0

--- a/solution.py
+++ b/solution.py
@@ -116,7 +116,7 @@
     )
     inner_step = jnp.sum(key_f * key_full, axis=2) - jnp.sum(query_f * query_full, axis=2)
     rate_part = jnp.sum(position[:, None] * inner_step, axis=0)
-    rate_total = lax.psum(rate_part, ("seq", "dp"))
+    rate_total = lax.psum(lax.psum(rate_part, "seq"), "dp")
     token_total = row_count * lax.axis_size("seq") * lax.axis_size("dp")
     rate_grad = head_decay_rate * rate_total / math.sqrt(token_total)
     out_shape = (1, row_count, HEADS * HEAD_DIM)

time: 649 us -> 661 us (1.018)
  blocking collectives: 157 us -> 169 us
    psum x1 -> x2, blocking collectives: 119 us -> 130 us  [on_device(): rate_total = lax.psum(lax.psum(rate_part, 'seq'), 'dp')]
where the time goes in v1:
time: 661 us; the launch traced here: 659 us
  waiting for transfers between devices  363 us (55%)
  blocking collectives  169 us (26%)
  other arithmetic  51.5 us (8%)
  matrix products  42 us (6%)
  local copies, waits for them, and re-layouts  17.7 us (3%)
  between operations  14.8 us (2%)
    all_gather x2, waiting for transfers between devices, carried_in(): gathered = jax.tree.map(lambda a: lax.all_gather(a, axis), part)  363 us
    psum x2, blocking collectives, on_device(): rate_total = lax.psum(lax.psum(rate_part, 'seq'), 'dp')  130 us
    add x31, other arithmetic, backward_combine(): later[1] + later[0][:, None, None] * earlier[1]  45.3 us
    all_gather x1, blocking collectives, carried_in(): gathered = jax.tree.map(lambda a: lax.all_gather(a, axis), part)  38.4 us
    unnamed x20, local copies, waits for them, and re-layouts  13.7 us
  transfers between devices with their start and end apart: 2, of which 2 were waited for; matrix products, arithmetic and copies ran while one was open for 10% of the time, Pallas kernels for 0%

profile of v1, /device:TPU:1, one launch (start us, length us, event | category | flops | bytes accessed | tf_op | source)
XLA Modules:
  0.0 659.1 jit_solution(1694882951233286263)
XLA Ops:
  13.9 1.9 copy.84
  15.8 2.4 copy.99
  18.5 2.4 fusion.9
  21.0 1.9 copy.81
  22.8 1.8 copy.101
  25.8 2.4 fusion.7
  28.2 38.4 %all-gather.2 = f32[32,1,16]{2,1,0:T(1,128)S(1)} all-gather(f32[1,1,16]{2,1,0:T(1,128)S(1)} %bitcast.115), channel_id=1, replica_groups=mesh['seq'=32,'dp'=8] {'seq'}, dimensions={0}, use_global_device_ids=true | all-gather | bytes 2112 | tf_op jit(solution)/shard_map/all_gather | solution.py:17
  66.9 6.9 %multiply_convert_fusion.1 = bf16[16,384,384]{2,1,0:T(8,128)(2,1)} fusion(f32[16,384]{1,0:T(8,128)S(1)} %get-tuple-element.184, pred[384,384]{1,0:T(8,128)(4,1)S(1)} %fusion.21, bf16[384,16,128]{0,2,1:T(8,128)(2,1)S(1)} %bitcast.99, bf16[384,16,128]{2,1,0:T(8,128)(2,1)} %bitcast.103), kind=kOutput, calls=%fused_computation.5 | convolution fusion | flops 615776256 | bytes 8036352 | tf_op jit(solution)/shard_map/shf,thf->hst/dot_general | solution.py:94
  73.8 184.0 %all-gather.8.cloned.1.call-done = f32[512,128,128]{2,1,0:T(8,128)} async-done(((f32[16,128,128]{2,1,0:T(8,128)}), f32[512,128,128]{2,1,0:T(8,128)}) %all-gather.8.cloned.1.call-update) | async-done | bytes 33554448 | tf_op jit(solution)/shard_map/all_gather | solution.py:17
  257.9 46.7 %while.27 = (s32[]{:T(128)}, f32[16,128,128]{2,1,0:T(8,128)S(1)}, s32[]{:T(128)}, f32[32,16,128,128]{3,2,1,0:T(8,128)}, f32[32,16]{1,0:T(8,128)S(1)}, /*index=5*/s32[]{:T(128)}, s32[]{:T(128)}, s32[]{:T(128)}, s32[]{:T(128)}) while((s32[]{:T(128)}, f32[16,128,128]{2,1,0:T(8,128)S(1)}, s32[]{:T(128)}, f32[32,16,128,128]{3,2,1,0:T(8,128)}, ...), condition=%wide.region_9.10_spmd, body=%wide.region_8.9_spmd.sunk | while | flops 524294 | bytes 3146075 | solution.py:26
  257.9 1.4 bitcast_add_fusion.5
  259.4 1.4 bitcast_add_fusion.5
  260.9 1.4 bitcast_add_fusion.5
  262.4 1.4 bitcast_add_fusion.5
  263.9 1.4 bitcast_add_fusion.5
  265.4 1.4 bitcast_add_fusion.5
  266.9 1.4 bitcast_add_fusion.5
  269.9 1.6 bitcast_add_fusion.5
  271.5 1.5 bitcast_add_fusion.5
  273.1 1.4 bitcast_add_fusion.5
  274.6 1.4 bitcast_add_fusion.5
  276.0 1.4 bitcast_add_fusion.5
  277.5 1.5 bitcast_add_fusion.5
  279.1 1.5 bitcast_add_fusion.5
  280.6 1.5 bitcast_add_fusion.5
  282.1 1.5 bitcast_add_fusion.5
  283.6 1.5 bitcast_add_fusion.5
  285.1 1.5 bitcast_add_fusion.5
  286.6 1.5 bitcast_add_fusion.5
  288.1 1.5 bitcast_add_fusion.5
  295.6 1.5 bitcast_add_fusion.5
  297.1 1.5 bitcast_add_fusion.5
  298.6 1.5 bitcast_add_fusion.5
  300.1 1.5 bitcast_add_fusion.5
  301.6 1.5 bitcast_add_fusion.5
  303.2 1.5 bitcast_add_fusion.5
  304.6 4.5 fusion.17
  309.2 2.7 fusion.25
  311.8 178.9 %all-gather.6.cloned.1.call-done = f32[512,128,128]{2,1,0:T(8,128)} async-done(((f32[16,128,128]{2,1,0:T(8,128)}), f32[512,128,128]{2,1,0:T(8,128)}) %all-gather.6.cloned.1.call-update) | async-done | bytes 33554448 | tf_op jit(solution)/shard_map/all_gather | solution.py:17
  491.1 4.0 fusion.24
  495.1 8.2 %fusion.12 = bf16[384,16,128]{0,2,1:T(8,128)(2,1)} fusion(f32[16,128,384]{2,1,0:T(8,128)} %fusion.25, bf16[384,16,128]{0,2,1:T(8,128)(2,1)} %bitcast.101, f32[16,384]{1,0:T(8,128)S(1)} %get-tuple-element.184, pred[384,384]{1,0:T(8,128)(4,1)S(1)} %fusion.21, bf16[384,16,128]{0,2,1:T(8,128)(2,1)} %bitcast.95, bf16[384,16,128]{0,2,1:T(8,128)(2,1)S(1)} %bitcast.91, ...), kind=kOutput, calls=%fused_computation.23 | convolution fusion | flops 1222115328 | bytes 9633792 | tf_op jit(solution)/shard_map/hst,shf->thf/dot_general | solution.py:99
  503.3 2.7 copy.94
  506.0 5.9 fusion.8
  512.0 5.1 fusion.10
  517.2 2.7 copy.92
  519.9 103.5 %psum.14 = f32[16]{0:T(128)S(1)} all-reduce(f32[16]{0:T(128)S(1)} %multiply_reduce_fusion), channel_id=1, replica_groups=mesh['seq'=32,'dp'=8] {'seq'}, use_global_device_ids=true, to_apply=%region_14.15 | all-reduce | flops 16 | bytes 128 | tf_op jit(solution)/shard_map/psum | solution.py:119
  623.4 26.7 %psum.15 = f32[16]{0:T(128)S(1)} all-reduce(f32[16]{0:T(128)S(1)} %psum.14), channel_id=1, replica_groups=mesh['seq'=32,'dp'=8] {'dp'}, use_global_device_ids=true, to_apply=%region_15.16 | all-reduce | flops 16 | bytes 128 | tf_op jit(solution)/shard_map/psum | solution.py:119
  650.6 1.6 copy.93
  (82 shorter events, 16.4 us)
Async XLA Ops:
  7.2 250.6 %all-gather.8.cloned.1.call-start = ((), (), s32[]{:S(2)}) async-start(), calls=%async_computation.1 | async-start | bytes 34603008 | tf_op jit(solution)/shard_map/all_gather | solution.py:17
  15.8 5.1 copy-start
  18.2 48.7 %copy-start.2 = (bf16[1,384,2048]{1,2,0:T(8,128)(2,1)}, bf16[1,384,2048]{1,2,0:T(8,128)(2,1)S(1)}, u32[]{:S(2)}) copy-start(bf16[1,384,2048]{1,2,0:T(8,128)(2,1)S(1)} %copy.99) | copy-start | bytes 4718596
  20.9 469.8 %all-gather.6.cloned.1.call-start = ((), (), s32[]{:S(2)}) async-start(), calls=%async_computation | async-start | bytes 34603008 | tf_op jit(solution)/shard_map/all_gather | solution.py:17
  24.7 1.1 copy-start.3
  503.3 2.7 copy-start.1
  506.0 5.9 copy-start.4
  517.1 133.1 %copy-start.6 = (f32[16]{0:T(128)S(1)}, f32[16]{0:T(128)}, u32[]{:S(2)}) copy-start(f32[16]{0:T(128)} %param.17) | copy-start | bytes 196
  517.1 133.6 %copy-start.5 = (bf16[384,16,128]{0,2,1:T(8,128)(2,1)S(1)}, bf16[384,16,128]{0,2,1:T(8,128)(2,1)}, u32[]{:S(2)}) copy-start(bf16[384,16,128]{0,2,1:T(8,128)(2,1)} %get-tuple-element.181) | copy-start | bytes 4718596
Sparse Core Ops, SparseCore 0:
  21.0 236.7 all-gather.7
  260.4 230.3 all-gather.5
